TPU v7x, 512 devices: a whole 4x8x8 slice. The times are simulated.
512 devices in a mesh: section: 8 (over x, core), tile: 64 (over z, y).
Axes of the slice: x: 4, y: 8, z: 8, core: 2. Of those that a mesh axis runs over, the one named last changes fastest.
Arguments:
- latents: bfloat16 [8, 2, 512, 384], P(None, None, 'tile'), may hold values from -6 to 6
- col_counts: int32 [64], replicated, may hold values from 1 to 8, 480 in all
- conv_weight: bfloat16 [8, 3, 3, 1152, 384], P('section'), may hold values from -0.0625 to 0.0625
- norm_gain: bfloat16 [8, 384], P('section'), may hold values from 0.099609375 to 1.8984375
Outputs:
- decoded: bfloat16 [8, 2, 512, 384], P('section', None, 'tile')
Inputs may be any that keep to these rules, and one draw needn't show every extreme that they name: Strip t holds col_counts[t] image columns; the counts sum to 480 and some strip holds 8.
All inputs are finite; a program needn't handle non-finite values.
Results may differ from a plain program's by a relative error of at most 0.013.
Values may be sent and summed in bfloat16 or wider, within the bound.
No kernel may reach another device: no remote copies, remote signals or barrier semaphores. Data moves between devices by JAX's collectives and lax.ppermute only.
A program may use at most 64 MiB of HBM per device.

v0:
```python
import jax
import jax.numpy as jnp
from jax import lax
from jax.sharding import PartitionSpec as P

SPAN_T = 4


def padded(block, sides, width):
    for axis, dim in sides:
        count = lax.axis_size(axis)
        forward = [(i, i + 1) for i in range(count - 1)]
        backward = [(target, source) for source, target in forward]
        low = lax.ppermute(
            lax.slice_in_dim(block, block.shape[dim] - width, None, axis=dim), axis, forward
        )
        high = lax.ppermute(lax.slice_in_dim(block, 0, width, axis=dim), axis, backward)
        block = jnp.concatenate([low, block, high], axis=dim)
    return block


def passed_along(block, axis, distance):
    devices = range(lax.axis_size(axis))
    route = [(i - distance, i) for i in devices if i - distance in devices]
    return lax.ppermute(block, axis, route)


def from_root(shard, axis, root):
    mine = lax.axis_index(axis) == root
    return lax.psum(jnp.where(mine, shard, jnp.zeros_like(shard)), axis)


def convolve(sequence, kernel, frame_depth, row_count, col_count):
    joined = jnp.concatenate(
        [
            sequence[:, :, 0:col_count],
            sequence[:, :, 1 : col_count + 1],
            sequence[:, :, 2 : col_count + 2],
        ],
        axis=-1,
    )
    summed = jnp.zeros((frame_depth, row_count, col_count, kernel.shape[-1]), jnp.float32)
    for frame_tap in range(3):
        for row_tap in range(3):
            summed = summed + jnp.dot(
                joined[frame_tap : frame_tap + frame_depth, row_tap : row_tap + row_count],
                kernel[frame_tap, row_tap],
                preferred_element_type=jnp.float32,
            )
    return summed


def local(latents, col_counts, conv_weight, norm_gain):
    segments = lax.axis_size("section")
    segment_index = lax.axis_index("section")
    tile_index = lax.axis_index("tile")
    frames_all, row_count, col_count, channels = latents.shape
    live_cols = col_counts[tile_index]
    kernel = conv_weight[0]
    norm_scale = norm_gain[0].astype(jnp.float32)
    frame_depth = SPAN_T
    pieces = frames_all // frame_depth
    total_steps = pieces + segments - 1
    col_live = jnp.arange(col_count)[None, None, :, None] < live_cols
    col_index = jnp.arange(col_count + 2)[None, None, :, None]
    even_segment = segment_index % 2 == 0
    last_segment = segment_index == segments - 1
    zero_value = jnp.zeros((), jnp.bfloat16)

    def advance(step_index, carried):
        inbound, memory, result = carried
        micro_index = step_index - segment_index
        active = (micro_index >= 0) & (micro_index < pieces)
        frame_start = jnp.clip(micro_index, 0, pieces - 1) * frame_depth
        entering = lax.dynamic_slice_in_dim(latents, frame_start, frame_depth, 0)
        residual = jnp.where(
            col_live, jnp.where(segment_index == 0, entering, inbound[0]), zero_value
        )
        branch = inbound[1]
        source = jnp.where(even_segment, residual, branch).astype(jnp.float32)
        normed = (
            source
            * lax.rsqrt(jnp.mean(source * source, axis=-1, keepdims=True) + 1e-06)
            * norm_scale
        )
        activated = jnp.where(col_live, jax.nn.silu(normed), 0.0).astype(jnp.bfloat16)
        first_col = activated[:, :, 0:1]
        last_col = lax.dynamic_slice_in_dim(activated, live_cols - 1, 1, 2)
        haloed = padded(jnp.concatenate([first_col, last_col], axis=2), (("tile", 2),), 1)
        widened = jnp.concatenate([haloed[:, :, 0:1], activated, jnp.zeros_like(first_col)], axis=2)
        widened = jnp.where(col_index == live_cols + 1, haloed[:, :, 3:4], widened)
        extended = jnp.pad(widened, ((0, 0), (1, 1), (0, 0), (0, 0)))
        sequence = jnp.concatenate([memory, extended], axis=0)
        memory = jnp.where(active, sequence[-2:], memory)
        conv_out = jnp.where(
            col_live, convolve(sequence, kernel, frame_depth, row_count, col_count), 0.0
        )
        resid_next = jnp.where(
            even_segment, residual, (residual.astype(jnp.float32) + conv_out).astype(jnp.bfloat16)
        )
        branch_next = jnp.where(even_segment, conv_out.astype(jnp.bfloat16), branch)
        written = lax.dynamic_update_slice_in_dim(result, resid_next, frame_start, 0)
        result = jnp.where(active & last_segment, written, result)
        inbound = passed_along(jnp.stack([resid_next, branch_next]), "section", 1)
        return (inbound, memory, result)

    inbound = jnp.zeros((2, frame_depth, row_count, col_count, channels), jnp.bfloat16)
    memory = jnp.zeros((2, row_count + 2, col_count + 2, channels), jnp.bfloat16)
    result = jnp.zeros((frames_all, row_count, col_count, channels), jnp.bfloat16)
    inbound, memory, result = lax.fori_loop(0, total_steps, advance, (inbound, memory, result))
    gathered = from_root(result, "section", segments - 1)
    frame_share = frames_all // segments
    return lax.dynamic_slice_in_dim(gathered, segment_index * frame_share, frame_share, 0)


def solution(mesh):
    return jax.shard_map(
        local,
        mesh=mesh,
        in_specs=(
            P(None, None, "tile", None),
            P(),
            P("section", None, None, None, None),
            P("section", None),
        ),
        out_specs=P("section", None, "tile", None),
        check_vma=False,
    )
```

profile of v0, /device:TPU:8, one launch (start us, length us, event | category | flops | bytes accessed | tf_op | source)
XLA Modules:
  0.0 376.8 jit_solution(10968144452210081428)
XLA Ops:
  10.5 269.9 %while.20 = (s32[]{:T(128)}, bf16[2,4,2,8,384]{4,3,2,1,0:T(8,128)(2,1)S(1)}, bf16[2,4,10,384]{3,2,1,0:T(8,128)(2,1)S(1)}, bf16[8,2,8,384]{3,2,1,0:T(8,128)(2,1)S...) while((s32[]{:T(128)}, ...), condition=%wide.region_2.3_spmd.clone, body=%wide.region_0.2_spmd.clone.sunk | while | flops 512637024 | bytes 16789532 | solution.py:110
  12.3 3.5 collective-permute-start
  15.8 5.5 %collective-permute-start.1 = (bf16[4,2,1,384]{3,2,1,0:T(2,128)(2,1)S(1)}, bf16[4,2,1,384]{3,2,1,0:T(2,128)(2,1)S(1)}, u32[]{:S(2)}, u32[]{:S(2)}) collective-permute-start(bf16[4,2,1,384]{3,2,1,0:T(2,128)(2,1)S(1)} %get-tuple-element.519), channel_id=1, source_target_pairs={{1,0},{2,1},{3,2},{4,3},{5,4},{6,5},{7,6},{8,7},{9,8},{10,9},{11,1... | collective-permute-start | bytes 18440 | tf_op jit(solution)/shard_map/while/body/eval_jaxpr/ppermute | solution.py:17
  26.0 1.4 convolution_add_fusion.16
  27.4 1.4 convolution_add_fusion.17
  28.8 1.4 convolution_add_fusion.18
  33.1 1.4 convolution_add_fusion.21
  34.6 1.5 select_dynamic-update-slice_fusion.2
  40.1 2.9 collective-permute-start
  43.0 2.9 collective-permute-start.1
  46.0 3.8 collective-permute-done.1
  54.5 1.4 convolution_add_fusion.17
  55.9 1.4 convolution_add_fusion.18
  60.2 1.4 convolution_add_fusion.21
  61.7 1.5 select_dynamic-update-slice_fusion.2
  63.2 3.7 collective-permute-start.2
  69.6 3.6 collective-permute-start
  73.2 2.2 collective-permute-start.1
  75.5 3.3 collective-permute-done.1
  83.5 1.4 convolution_add_fusion.17
  84.9 1.4 convolution_add_fusion.18
  89.2 1.4 convolution_add_fusion.21
  90.6 1.5 select_dynamic-update-slice_fusion.2
  92.1 5.0 %collective-permute-start.2 = (bf16[2,4,2,8,384]{4,3,2,1,0:T(8,128)(2,1)S(1)}, bf16[2,4,2,8,384]{4,3,2,1,0:T(8,128)(2,1)S(1)}, u32[]{:S(2)}, u32[]{:S(2)}) collective-permute-start(bf16[2,4,2,8,384]{4,3,2,1,0:T(8,128)(2,1)S(1)} %pad_maximum_fusion.3), channel_id=1, source_target_pairs={{0,64},{64,128},{128,192},{192,256},{256,320},{320,384},{384,448},... | collective-permute-start | bytes 294920 | tf_op jit(solution)/shard_map/while/body/eval_jaxpr/ppermute | solution.py:25
  99.9 3.1 collective-permute-start
  103.0 2.7 collective-permute-start.1
  105.8 2.8 collective-permute-done.1
  110.4 1.4 convolution_add_fusion.15
  111.9 1.4 convolution_add_fusion.16
  113.3 1.4 convolution_add_fusion.17
  117.6 1.4 convolution_add_fusion.20
  119.0 1.4 convolution_add_fusion.21
  120.5 1.5 select_dynamic-update-slice_fusion.2
  121.9 5.0 %collective-permute-start.2 = (bf16[2,4,2,8,384]{4,3,2,1,0:T(8,128)(2,1)S(1)}, bf16[2,4,2,8,384]{4,3,2,1,0:T(8,128)(2,1)S(1)}, u32[]{:S(2)}, u32[]{:S(2)}) collective-permute-start(bf16[2,4,2,8,384]{4,3,2,1,0:T(8,128)(2,1)S(1)} %pad_maximum_fusion.3), channel_id=1, source_target_pairs={{0,64},{64,128},{128,192},{192,256},{256,320},{320,384},{384,448},... | collective-permute-start | bytes 294920 | tf_op jit(solution)/shard_map/while/body/eval_jaxpr/ppermute | solution.py:25
  129.7 3.1 collective-permute-start
  132.8 2.7 collective-permute-start.1
  135.6 2.8 collective-permute-done.1
  140.3 1.4 convolution_add_fusion.15
  144.5 1.4 convolution_add_fusion.18
  146.0 1.4 convolution_add_fusion.19
  150.3 1.5 select_dynamic-update-slice_fusion.2
  151.8 5.0 %collective-permute-start.2 = (bf16[2,4,2,8,384]{4,3,2,1,0:T(8,128)(2,1)S(1)}, bf16[2,4,2,8,384]{4,3,2,1,0:T(8,128)(2,1)S(1)}, u32[]{:S(2)}, u32[]{:S(2)}) collective-permute-start(bf16[2,4,2,8,384]{4,3,2,1,0:T(8,128)(2,1)S(1)} %pad_maximum_fusion.3), channel_id=1, source_target_pairs={{0,64},{64,128},{128,192},{192,256},{256,320},{320,384},{384,448},... | collective-permute-start | bytes 294920 | tf_op jit(solution)/shard_map/while/body/eval_jaxpr/ppermute | solution.py:25
  159.5 3.2 collective-permute-start
  162.7 2.7 collective-permute-start.1
  165.4 2.9 collective-permute-done.1
  180.2 1.5 select_dynamic-update-slice_fusion.2
  181.7 5.3 %collective-permute-start.2 = (bf16[2,4,2,8,384]{4,3,2,1,0:T(8,128)(2,1)S(1)}, bf16[2,4,2,8,384]{4,3,2,1,0:T(8,128)(2,1)S(1)}, u32[]{:S(2)}, u32[]{:S(2)}) collective-permute-start(bf16[2,4,2,8,384]{4,3,2,1,0:T(8,128)(2,1)S(1)} %pad_maximum_fusion.3), channel_id=1, source_target_pairs={{0,64},{64,128},{128,192},{192,256},{256,320},{320,384},{384,448},... | collective-permute-start | bytes 294920 | tf_op jit(solution)/shard_map/while/body/eval_jaxpr/ppermute | solution.py:25
  189.7 3.6 collective-permute-start
  193.4 2.2 collective-permute-start.1
  195.7 3.4 collective-permute-done.1
  210.9 1.5 select_dynamic-update-slice_fusion.2
  212.4 5.3 %collective-permute-start.2 = (bf16[2,4,2,8,384]{4,3,2,1,0:T(8,128)(2,1)S(1)}, bf16[2,4,2,8,384]{4,3,2,1,0:T(8,128)(2,1)S(1)}, u32[]{:S(2)}, u32[]{:S(2)}) collective-permute-start(bf16[2,4,2,8,384]{4,3,2,1,0:T(8,128)(2,1)S(1)} %pad_maximum_fusion.3), channel_id=1, source_target_pairs={{0,64},{64,128},{128,192},{192,256},{256,320},{320,384},{384,448},... | collective-permute-start | bytes 294920 | tf_op jit(solution)/shard_map/while/body/eval_jaxpr/ppermute | solution.py:25
  220.4 3.6 collective-permute-start
  224.1 2.2 collective-permute-start.1
  226.4 3.7 collective-permute-done.1
  242.0 1.5 select_dynamic-update-slice_fusion.2
  243.5 5.3 %collective-permute-start.2 = (bf16[2,4,2,8,384]{4,3,2,1,0:T(8,128)(2,1)S(1)}, bf16[2,4,2,8,384]{4,3,2,1,0:T(8,128)(2,1)S(1)}, u32[]{:S(2)}, u32[]{:S(2)}) collective-permute-start(bf16[2,4,2,8,384]{4,3,2,1,0:T(8,128)(2,1)S(1)} %pad_maximum_fusion.3), channel_id=1, source_target_pairs={{0,64},{64,128},{128,192},{192,256},{256,320},{320,384},{384,448},... | collective-permute-start | bytes 294920 | tf_op jit(solution)/shard_map/while/body/eval_jaxpr/ppermute | solution.py:25
  251.5 3.6 collective-permute-start
  255.1 2.2 collective-permute-start.1
  257.4 3.4 collective-permute-done.1
  271.2 1.4 convolution_add_fusion.21
  272.7 1.5 select_dynamic-update-slice_fusion.2
  274.2 5.3 %collective-permute-start.2 = (bf16[2,4,2,8,384]{4,3,2,1,0:T(8,128)(2,1)S(1)}, bf16[2,4,2,8,384]{4,3,2,1,0:T(8,128)(2,1)S(1)}, u32[]{:S(2)}, u32[]{:S(2)}) collective-permute-start(bf16[2,4,2,8,384]{4,3,2,1,0:T(8,128)(2,1)S(1)} %pad_maximum_fusion.3), channel_id=1, source_target_pairs={{0,64},{64,128},{128,192},{192,256},{256,320},{320,384},{384,448},... | collective-permute-start | bytes 294920 | tf_op jit(solution)/shard_map/while/body/eval_jaxpr/ppermute | solution.py:25
  281.1 87.6 %all-reduce.3.cloned.1.call-done = bf16[8,2,8,384]{3,2,1,0:T(8,128)(2,1)} async-done(((bf16[8,2,8,384]{3,2,1,0:T(8,128)(2,1)}), bf16[8,2,8,384]{3,2,1,0:T(8,128)(2,1)}) %all-reduce.3.cloned.1.call-update) | async-done | bytes 98320 | tf_op jit(solution)/shard_map/psum | solution.py:30
  (208 shorter events, 110.3 us)
Async XLA Ops:
  6.5 362.1 %all-reduce.3.cloned.1.call-start = ((), (), s32[]{:S(2)}) async-start(), calls=%async_computation | async-start | bytes 196608 | tf_op jit(solution)/shard_map/psum | solution.py:30
  12.3 10.4 %collective-permute-start = (bf16[4,2,1,384]{3,2,1,0:T(2,128)(2,1)S(1)}, bf16[4,2,1,384]{3,2,1,0:T(2,128)(2,1)S(1)}, u32[]{:S(2)}, u32[]{:S(2)}) collective-permute-start(bf16[4,2,1,384]{3,2,1,0:T(2,128)(2,1)S(1)} %get-tuple-element.518), channel_id=1, source_target_pairs={{0,1},{1,2},{2,3},{3,4},{4,5},{5,6},{6,7},{7,8},{8,9},{9,10},{10,1... | collective-permute-start | bytes 18440 | tf_op jit(solution)/shard_map/while/body/eval_jaxpr/ppermute | solution.py:14
  15.8 6.9 %collective-permute-start.1 = (bf16[4,2,1,384]{3,2,1,0:T(2,128)(2,1)S(1)}, bf16[4,2,1,384]{3,2,1,0:T(2,128)(2,1)S(1)}, u32[]{:S(2)}, u32[]{:S(2)}) collective-permute-start(bf16[4,2,1,384]{3,2,1,0:T(2,128)(2,1)S(1)} %get-tuple-element.519), channel_id=1, source_target_pairs={{1,0},{2,1},{3,2},{4,3},{5,4},{6,5},{7,6},{8,7},{9,8},{10,9},{11,1... | collective-permute-start | bytes 18440 | tf_op jit(solution)/shard_map/while/body/eval_jaxpr/ppermute | solution.py:17
  36.1 2.2 collective-permute-start.2
  40.1 9.7 %collective-permute-start = (bf16[4,2,1,384]{3,2,1,0:T(2,128)(2,1)S(1)}, bf16[4,2,1,384]{3,2,1,0:T(2,128)(2,1)S(1)}, u32[]{:S(2)}, u32[]{:S(2)}) collective-permute-start(bf16[4,2,1,384]{3,2,1,0:T(2,128)(2,1)S(1)} %get-tuple-element.518), channel_id=1, source_target_pairs={{0,1},{1,2},{2,3},{3,4},{4,5},{5,6},{6,7},{7,8},{8,9},{9,10},{10,1... | collective-permute-start | bytes 18440 | tf_op jit(solution)/shard_map/while/body/eval_jaxpr/ppermute | solution.py:14
  43.0 6.8 %collective-permute-start.1 = (bf16[4,2,1,384]{3,2,1,0:T(2,128)(2,1)S(1)}, bf16[4,2,1,384]{3,2,1,0:T(2,128)(2,1)S(1)}, u32[]{:S(2)}, u32[]{:S(2)}) collective-permute-start(bf16[4,2,1,384]{3,2,1,0:T(2,128)(2,1)S(1)} %get-tuple-element.519), channel_id=1, source_target_pairs={{1,0},{2,1},{3,2},{4,3},{5,4},{6,5},{7,6},{8,7},{9,8},{10,9},{11,1... | collective-permute-start | bytes 18440 | tf_op jit(solution)/shard_map/while/body/eval_jaxpr/ppermute | solution.py:17
  63.2 4.6 %collective-permute-start.2 = (bf16[2,4,2,8,384]{4,3,2,1,0:T(8,128)(2,1)S(1)}, bf16[2,4,2,8,384]{4,3,2,1,0:T(8,128)(2,1)S(1)}, u32[]{:S(2)}, u32[]{:S(2)}) collective-permute-start(bf16[2,4,2,8,384]{4,3,2,1,0:T(8,128)(2,1)S(1)} %pad_maximum_fusion.3), channel_id=1, source_target_pairs={{0,64},{64,128},{128,192},{192,256},{256,320},{320,384},{384,448},... | collective-permute-start | bytes 294920 | tf_op jit(solution)/shard_map/while/body/eval_jaxpr/ppermute | solution.py:25
  69.6 9.3 %collective-permute-start = (bf16[4,2,1,384]{3,2,1,0:T(2,128)(2,1)S(1)}, bf16[4,2,1,384]{3,2,1,0:T(2,128)(2,1)S(1)}, u32[]{:S(2)}, u32[]{:S(2)}) collective-permute-start(bf16[4,2,1,384]{3,2,1,0:T(2,128)(2,1)S(1)} %get-tuple-element.518), channel_id=1, source_target_pairs={{0,1},{1,2},{2,3},{3,4},{4,5},{5,6},{6,7},{7,8},{8,9},{9,10},{10,1... | collective-permute-start | bytes 18440 | tf_op jit(solution)/shard_map/while/body/eval_jaxpr/ppermute | solution.py:14
  73.2 5.6 %collective-permute-start.1 = (bf16[4,2,1,384]{3,2,1,0:T(2,128)(2,1)S(1)}, bf16[4,2,1,384]{3,2,1,0:T(2,128)(2,1)S(1)}, u32[]{:S(2)}, u32[]{:S(2)}) collective-permute-start(bf16[4,2,1,384]{3,2,1,0:T(2,128)(2,1)S(1)} %get-tuple-element.519), channel_id=1, source_target_pairs={{1,0},{2,1},{3,2},{4,3},{5,4},{6,5},{7,6},{8,7},{9,8},{10,9},{11,1... | collective-permute-start | bytes 18440 | tf_op jit(solution)/shard_map/while/body/eval_jaxpr/ppermute | solution.py:17
  92.1 5.9 %collective-permute-start.2 = (bf16[2,4,2,8,384]{4,3,2,1,0:T(8,128)(2,1)S(1)}, bf16[2,4,2,8,384]{4,3,2,1,0:T(8,128)(2,1)S(1)}, u32[]{:S(2)}, u32[]{:S(2)}) collective-permute-start(bf16[2,4,2,8,384]{4,3,2,1,0:T(8,128)(2,1)S(1)} %pad_maximum_fusion.3), channel_id=1, source_target_pairs={{0,64},{64,128},{128,192},{192,256},{256,320},{320,384},{384,448},... | collective-permute-start | bytes 294920 | tf_op jit(solution)/shard_map/while/body/eval_jaxpr/ppermute | solution.py:25
  99.9 8.7 %collective-permute-start = (bf16[4,2,1,384]{3,2,1,0:T(2,128)(2,1)S(1)}, bf16[4,2,1,384]{3,2,1,0:T(2,128)(2,1)S(1)}, u32[]{:S(2)}, u32[]{:S(2)}) collective-permute-start(bf16[4,2,1,384]{3,2,1,0:T(2,128)(2,1)S(1)} %get-tuple-element.518), channel_id=1, source_target_pairs={{0,1},{1,2},{2,3},{3,4},{4,5},{5,6},{6,7},{7,8},{8,9},{9,10},{10,1... | collective-permute-start | bytes 18440 | tf_op jit(solution)/shard_map/while/body/eval_jaxpr/ppermute | solution.py:14
  103.0 5.6 %collective-permute-start.1 = (bf16[4,2,1,384]{3,2,1,0:T(2,128)(2,1)S(1)}, bf16[4,2,1,384]{3,2,1,0:T(2,128)(2,1)S(1)}, u32[]{:S(2)}, u32[]{:S(2)}) collective-permute-start(bf16[4,2,1,384]{3,2,1,0:T(2,128)(2,1)S(1)} %get-tuple-element.519), channel_id=1, source_target_pairs={{1,0},{2,1},{3,2},{4,3},{5,4},{6,5},{7,6},{8,7},{9,8},{10,9},{11,1... | collective-permute-start | bytes 18440 | tf_op jit(solution)/shard_map/while/body/eval_jaxpr/ppermute | solution.py:17
  121.9 5.9 %collective-permute-start.2 = (bf16[2,4,2,8,384]{4,3,2,1,0:T(8,128)(2,1)S(1)}, bf16[2,4,2,8,384]{4,3,2,1,0:T(8,128)(2,1)S(1)}, u32[]{:S(2)}, u32[]{:S(2)}) collective-permute-start(bf16[2,4,2,8,384]{4,3,2,1,0:T(8,128)(2,1)S(1)} %pad_maximum_fusion.3), channel_id=1, source_target_pairs={{0,64},{64,128},{128,192},{192,256},{256,320},{320,384},{384,448},... | collective-permute-start | bytes 294920 | tf_op jit(solution)/shard_map/while/body/eval_jaxpr/ppermute | solution.py:25
  129.7 8.7 %collective-permute-start = (bf16[4,2,1,384]{3,2,1,0:T(2,128)(2,1)S(1)}, bf16[4,2,1,384]{3,2,1,0:T(2,128)(2,1)S(1)}, u32[]{:S(2)}, u32[]{:S(2)}) collective-permute-start(bf16[4,2,1,384]{3,2,1,0:T(2,128)(2,1)S(1)} %get-tuple-element.518), channel_id=1, source_target_pairs={{0,1},{1,2},{2,3},{3,4},{4,5},{5,6},{6,7},{7,8},{8,9},{9,10},{10,1... | collective-permute-start | bytes 18440 | tf_op jit(solution)/shard_map/while/body/eval_jaxpr/ppermute | solution.py:14
  132.8 5.6 %collective-permute-start.1 = (bf16[4,2,1,384]{3,2,1,0:T(2,128)(2,1)S(1)}, bf16[4,2,1,384]{3,2,1,0:T(2,128)(2,1)S(1)}, u32[]{:S(2)}, u32[]{:S(2)}) collective-permute-start(bf16[4,2,1,384]{3,2,1,0:T(2,128)(2,1)S(1)} %get-tuple-element.519), channel_id=1, source_target_pairs={{1,0},{2,1},{3,2},{4,3},{5,4},{6,5},{7,6},{8,7},{9,8},{10,9},{11,1... | collective-permute-start | bytes 18440 | tf_op jit(solution)/shard_map/while/body/eval_jaxpr/ppermute | solution.py:17
  151.8 5.9 %collective-permute-start.2 = (bf16[2,4,2,8,384]{4,3,2,1,0:T(8,128)(2,1)S(1)}, bf16[2,4,2,8,384]{4,3,2,1,0:T(8,128)(2,1)S(1)}, u32[]{:S(2)}, u32[]{:S(2)}) collective-permute-start(bf16[2,4,2,8,384]{4,3,2,1,0:T(8,128)(2,1)S(1)} %pad_maximum_fusion.3), channel_id=1, source_target_pairs={{0,64},{64,128},{128,192},{192,256},{256,320},{320,384},{384,448},... | collective-permute-start | bytes 294920 | tf_op jit(solution)/shard_map/while/body/eval_jaxpr/ppermute | solution.py:25
  159.5 8.9 %collective-permute-start = (bf16[4,2,1,384]{3,2,1,0:T(2,128)(2,1)S(1)}, bf16[4,2,1,384]{3,2,1,0:T(2,128)(2,1)S(1)}, u32[]{:S(2)}, u32[]{:S(2)}) collective-permute-start(bf16[4,2,1,384]{3,2,1,0:T(2,128)(2,1)S(1)} %get-tuple-element.518), channel_id=1, source_target_pairs={{0,1},{1,2},{2,3},{3,4},{4,5},{5,6},{6,7},{7,8},{8,9},{9,10},{10,1... | collective-permute-start | bytes 18440 | tf_op jit(solution)/shard_map/while/body/eval_jaxpr/ppermute | solution.py:14
  162.7 5.7 %collective-permute-start.1 = (bf16[4,2,1,384]{3,2,1,0:T(2,128)(2,1)S(1)}, bf16[4,2,1,384]{3,2,1,0:T(2,128)(2,1)S(1)}, u32[]{:S(2)}, u32[]{:S(2)}) collective-permute-start(bf16[4,2,1,384]{3,2,1,0:T(2,128)(2,1)S(1)} %get-tuple-element.519), channel_id=1, source_target_pairs={{1,0},{2,1},{3,2},{4,3},{5,4},{6,5},{7,6},{8,7},{9,8},{10,9},{11,1... | collective-permute-start | bytes 18440 | tf_op jit(solution)/shard_map/while/body/eval_jaxpr/ppermute | solution.py:17
  181.7 6.2 %collective-permute-start.2 = (bf16[2,4,2,8,384]{4,3,2,1,0:T(8,128)(2,1)S(1)}, bf16[2,4,2,8,384]{4,3,2,1,0:T(8,128)(2,1)S(1)}, u32[]{:S(2)}, u32[]{:S(2)}) collective-permute-start(bf16[2,4,2,8,384]{4,3,2,1,0:T(8,128)(2,1)S(1)} %pad_maximum_fusion.3), channel_id=1, source_target_pairs={{0,64},{64,128},{128,192},{192,256},{256,320},{320,384},{384,448},... | collective-permute-start | bytes 294920 | tf_op jit(solution)/shard_map/while/body/eval_jaxpr/ppermute | solution.py:25
  189.7 9.4 %collective-permute-start = (bf16[4,2,1,384]{3,2,1,0:T(2,128)(2,1)S(1)}, bf16[4,2,1,384]{3,2,1,0:T(2,128)(2,1)S(1)}, u32[]{:S(2)}, u32[]{:S(2)}) collective-permute-start(bf16[4,2,1,384]{3,2,1,0:T(2,128)(2,1)S(1)} %get-tuple-element.518), channel_id=1, source_target_pairs={{0,1},{1,2},{2,3},{3,4},{4,5},{5,6},{6,7},{7,8},{8,9},{9,10},{10,1... | collective-permute-start | bytes 18440 | tf_op jit(solution)/shard_map/while/body/eval_jaxpr/ppermute | solution.py:14
  193.4 5.7 %collective-permute-start.1 = (bf16[4,2,1,384]{3,2,1,0:T(2,128)(2,1)S(1)}, bf16[4,2,1,384]{3,2,1,0:T(2,128)(2,1)S(1)}, u32[]{:S(2)}, u32[]{:S(2)}) collective-permute-start(bf16[4,2,1,384]{3,2,1,0:T(2,128)(2,1)S(1)} %get-tuple-element.519), channel_id=1, source_target_pairs={{1,0},{2,1},{3,2},{4,3},{5,4},{6,5},{7,6},{8,7},{9,8},{10,9},{11,1... | collective-permute-start | bytes 18440 | tf_op jit(solution)/shard_map/while/body/eval_jaxpr/ppermute | solution.py:17
  212.4 6.2 %collective-permute-start.2 = (bf16[2,4,2,8,384]{4,3,2,1,0:T(8,128)(2,1)S(1)}, bf16[2,4,2,8,384]{4,3,2,1,0:T(8,128)(2,1)S(1)}, u32[]{:S(2)}, u32[]{:S(2)}) collective-permute-start(bf16[2,4,2,8,384]{4,3,2,1,0:T(8,128)(2,1)S(1)} %pad_maximum_fusion.3), channel_id=1, source_target_pairs={{0,64},{64,128},{128,192},{192,256},{256,320},{320,384},{384,448},... | collective-permute-start | bytes 294920 | tf_op jit(solution)/shard_map/while/body/eval_jaxpr/ppermute | solution.py:25
  220.4 9.7 %collective-permute-start = (bf16[4,2,1,384]{3,2,1,0:T(2,128)(2,1)S(1)}, bf16[4,2,1,384]{3,2,1,0:T(2,128)(2,1)S(1)}, u32[]{:S(2)}, u32[]{:S(2)}) collective-permute-start(bf16[4,2,1,384]{3,2,1,0:T(2,128)(2,1)S(1)} %get-tuple-element.518), channel_id=1, source_target_pairs={{0,1},{1,2},{2,3},{3,4},{4,5},{5,6},{6,7},{7,8},{8,9},{9,10},{10,1... | collective-permute-start | bytes 18440 | tf_op jit(solution)/shard_map/while/body/eval_jaxpr/ppermute | solution.py:14
  224.1 6.0 %collective-permute-start.1 = (bf16[4,2,1,384]{3,2,1,0:T(2,128)(2,1)S(1)}, bf16[4,2,1,384]{3,2,1,0:T(2,128)(2,1)S(1)}, u32[]{:S(2)}, u32[]{:S(2)}) collective-permute-start(bf16[4,2,1,384]{3,2,1,0:T(2,128)(2,1)S(1)} %get-tuple-element.519), channel_id=1, source_target_pairs={{1,0},{2,1},{3,2},{4,3},{5,4},{6,5},{7,6},{8,7},{9,8},{10,9},{11,1... | collective-permute-start | bytes 18440 | tf_op jit(solution)/shard_map/while/body/eval_jaxpr/ppermute | solution.py:17
  243.5 6.2 %collective-permute-start.2 = (bf16[2,4,2,8,384]{4,3,2,1,0:T(8,128)(2,1)S(1)}, bf16[2,4,2,8,384]{4,3,2,1,0:T(8,128)(2,1)S(1)}, u32[]{:S(2)}, u32[]{:S(2)}) collective-permute-start(bf16[2,4,2,8,384]{4,3,2,1,0:T(8,128)(2,1)S(1)} %pad_maximum_fusion.3), channel_id=1, source_target_pairs={{0,64},{64,128},{128,192},{192,256},{256,320},{320,384},{384,448},... | collective-permute-start | bytes 294920 | tf_op jit(solution)/shard_map/while/body/eval_jaxpr/ppermute | solution.py:25
  251.5 9.4 %collective-permute-start = (bf16[4,2,1,384]{3,2,1,0:T(2,128)(2,1)S(1)}, bf16[4,2,1,384]{3,2,1,0:T(2,128)(2,1)S(1)}, u32[]{:S(2)}, u32[]{:S(2)}) collective-permute-start(bf16[4,2,1,384]{3,2,1,0:T(2,128)(2,1)S(1)} %get-tuple-element.518), channel_id=1, source_target_pairs={{0,1},{1,2},{2,3},{3,4},{4,5},{5,6},{6,7},{7,8},{8,9},{9,10},{10,1... | collective-permute-start | bytes 18440 | tf_op jit(solution)/shard_map/while/body/eval_jaxpr/ppermute | solution.py:14
  255.1 5.7 %collective-permute-start.1 = (bf16[4,2,1,384]{3,2,1,0:T(2,128)(2,1)S(1)}, bf16[4,2,1,384]{3,2,1,0:T(2,128)(2,1)S(1)}, u32[]{:S(2)}, u32[]{:S(2)}) collective-permute-start(bf16[4,2,1,384]{3,2,1,0:T(2,128)(2,1)S(1)} %get-tuple-element.519), channel_id=1, source_target_pairs={{1,0},{2,1},{3,2},{4,3},{5,4},{6,5},{7,6},{8,7},{9,8},{10,9},{11,1... | collective-permute-start | bytes 18440 | tf_op jit(solution)/shard_map/while/body/eval_jaxpr/ppermute | solution.py:17
  274.2 6.2 %collective-permute-start.2 = (bf16[2,4,2,8,384]{4,3,2,1,0:T(8,128)(2,1)S(1)}, bf16[2,4,2,8,384]{4,3,2,1,0:T(8,128)(2,1)S(1)}, u32[]{:S(2)}, u32[]{:S(2)}) collective-permute-start(bf16[2,4,2,8,384]{4,3,2,1,0:T(8,128)(2,1)S(1)} %pad_maximum_fusion.3), channel_id=1, source_target_pairs={{0,64},{64,128},{128,192},{192,256},{256,320},{320,384},{384,448},... | collective-permute-start | bytes 294920 | tf_op jit(solution)/shard_map/while/body/eval_jaxpr/ppermute | solution.py:25
Sparse Core Ops, SparseCore 0:
  281.2 87.4 all-reduce.2
where the time goes:
time: 382 us; the launch traced here: 377 us
  waiting for transfers between devices  123 us (32%)
  matrix products  116 us (30%)
  starting transfers between devices  96.9 us (25%)
  other arithmetic  20.4 us (5%)
  between operations  15.3 us (4%)
    dot_general x81, matrix products, convolve(): jnp.dot(joined[frame_tap:frame_tap + frame_depth, row_tap:row_tap + row_c...  116 us
    psum x1, waiting for transfers between devices, from_root(): return lax.psum(jnp.where(mine, shard, jnp.zeros_like(shard)), axis)  87.6 us
    ppermute x9, starting transfers between devices, passed_along(): return lax.ppermute(block, axis, route)  41.1 us
    ppermute x9, starting transfers between devices, padded(): lax.ppermute(lax.slice_in_dim(block, block.shape[dim] - width, None, axis...  30.4 us
    ppermute x9, waiting for transfers between devices, padded(): lax.ppermute(lax.slice_in_dim(block, 0, width, axis=dim), axis, backward)  27.2 us
    ppermute x9, starting transfers between devices, padded(): lax.ppermute(lax.slice_in_dim(block, 0, width, axis=dim), axis, backward)  25.3 us
    reduce_sum x9, other arithmetic, advance(): jnp.mean(source * source, axis=-1, keepdims=True) + 1e-06  8.76 us
    ppermute x9, waiting for transfers between devices, passed_along(): return lax.ppermute(block, axis, route)  8.26 us
  transfers between devices with their start and end apart: 28, of which 19 were waited for; matrix products, arithmetic and copies ran while one was open for 0% of the time, Pallas kernels for 0%

commit v1 on v0

--- a/solution.py
+++ b/solution.py
@@ -4,6 +4,10 @@
 from jax.sharding import PartitionSpec as P
 
 SPAN_T = 4
+
+
+def create_lines_in(raw, chip_axis):
+    return lax.all_gather(raw, axis_name=chip_axis).sum(axis=0)
 
 
 def padded(block, sides, width):
@@ -27,7 +31,7 @@
 
 def from_root(shard, axis, root):
     mine = lax.axis_index(axis) == root
-    return lax.psum(jnp.where(mine, shard, jnp.zeros_like(shard)), axis)
+    return create_lines_in(jnp.where(mine, shard, jnp.zeros_like(shard)), axis)
 
 
 def convolve(sequence, kernel, frame_depth, row_count, col_count):

time: 382 us -> 314 us (0.82)
  the two profiles are of different devices: /device:TPU:8 before, /device:TPU:249 now
where the time goes in v1:
time: 314 us; the launch traced here: 309 us
  matrix products  116 us (37%)
  starting transfers between devices  97.4 us (31%)
  waiting for transfers between devices  54.5 us (17%)
  other arithmetic  19.7 us (6%)
  blocking collectives  15 us (5%)
    dot_general x81, matrix products, convolve(): jnp.dot(joined[frame_tap:frame_tap + frame_depth, row_tap:row_tap + row_c...  116 us
    ppermute x9, starting transfers between devices, passed_along(): return lax.ppermute(block, axis, route)  48.8 us
    ppermute x9, waiting for transfers between devices, padded(): lax.ppermute(lax.slice_in_dim(block, 0, width, axis=dim), axis, backward)  39.9 us
    ppermute x9, starting transfers between devices, padded(): lax.ppermute(lax.slice_in_dim(block, 0, width, axis=dim), axis, backward)  28.8 us
    ppermute x9, starting transfers between devices, padded(): lax.ppermute(lax.slice_in_dim(block, block.shape[dim] - width, None, axis...  19.8 us
    all_gather x1, blocking collectives, create_lines_in(): return lax.all_gather(raw, axis_name=chip_axis).sum(axis=0)  15 us
    ppermute x9, waiting for transfers between devices, passed_along(): return lax.ppermute(block, axis, route)  14.5 us
    reduce_sum x9, other arithmetic, advance(): jnp.mean(source * source, axis=-1, keepdims=True) + 1e-06  8.75 us
  transfers between devices with their start and end apart: 27, of which 18 were waited for; matrix products, arithmetic and copies ran while one was open for 0% of the time, Pallas kernels for 0%

profile of v1, /device:TPU:249, one launch (start us, length us, event | category | flops | bytes accessed | tf_op | source)
XLA Modules:
  0.0 308.8 jit_solution(3780561047105611739)
XLA Ops:
  3.9 289.2 %while.20 = (s32[]{:T(128)}, bf16[2,4,2,8,384]{4,3,2,1,0:T(8,128)(2,1)S(1)}, bf16[2,4,10,384]{3,2,1,0:T(8,128)(2,1)S(1)}, bf16[8,2,8,384]{3,2,1,0:T(8,128)(2,1)S...) while((s32[]{:T(128)}, ...), condition=%wide.region_2.3_spmd.clone, body=%wide.region_0.2_spmd.clone.sunk | while | flops 512637024 | bytes 16789532 | solution.py:114
  5.6 4.4 %collective-permute-start = (bf16[4,2,1,384]{3,2,1,0:T(2,128)(2,1)S(1)}, bf16[4,2,1,384]{3,2,1,0:T(2,128)(2,1)S(1)}, u32[]{:S(2)}, u32[]{:S(2)}) collective-permute-start(bf16[4,2,1,384]{3,2,1,0:T(2,128)(2,1)S(1)} %get-tuple-element.518), channel_id=1, source_target_pairs={{0,1},{1,2},{2,3},{3,4},{4,5},{5,6},{6,7},{7,8},{8,9},{9,10},{10,1... | collective-permute-start | bytes 18440 | tf_op jit(solution)/shard_map/while/body/eval_jaxpr/ppermute | solution.py:18
  10.1 1.9 collective-permute-start.1
  12.1 5.7 %collective-permute-done.1 = bf16[4,2,1,384]{3,2,1,0:T(2,128)(2,1)S(1)} collective-permute-done((bf16[4,2,1,384]{3,2,1,0:T(2,128)(2,1)S(1)}, bf16[4,2,1,384]{3,2,1,0:T(2,128)(2,1)S(1)}, u32[]{:S(2)}, u32[]{:S(2)}) %collective-permute-start.1) | collective-permute-done | bytes 6176 | tf_op jit(solution)/shard_map/while/body/eval_jaxpr/ppermute | solution.py:21
  21.1 1.4 convolution_add_fusion.16
  22.5 1.4 convolution_add_fusion.17
  26.8 1.4 convolution_add_fusion.20
  28.3 1.4 convolution_add_fusion.21
  29.7 1.5 select_dynamic-update-slice_fusion.2
  31.2 5.1 %collective-permute-start.2 = (bf16[2,4,2,8,384]{4,3,2,1,0:T(8,128)(2,1)S(1)}, bf16[2,4,2,8,384]{4,3,2,1,0:T(8,128)(2,1)S(1)}, u32[]{:S(2)}, u32[]{:S(2)}) collective-permute-start(bf16[2,4,2,8,384]{4,3,2,1,0:T(8,128)(2,1)S(1)} %pad_maximum_fusion.3), channel_id=1, source_target_pairs={{0,64},{64,128},{128,192},{192,256},{256,320},{320,384},{384,448},... | collective-permute-start | bytes 294920 | tf_op jit(solution)/shard_map/while/body/eval_jaxpr/ppermute | solution.py:29
  36.3 1.6 collective-permute-done.2
  39.7 1.9 collective-permute-start
  41.6 3.4 %collective-permute-start.1 = (bf16[4,2,1,384]{3,2,1,0:T(2,128)(2,1)S(1)}, bf16[4,2,1,384]{3,2,1,0:T(2,128)(2,1)S(1)}, u32[]{:S(2)}, u32[]{:S(2)}) collective-permute-start(bf16[4,2,1,384]{3,2,1,0:T(2,128)(2,1)S(1)} %get-tuple-element.519), channel_id=1, source_target_pairs={{1,0},{2,1},{3,2},{4,3},{5,4},{6,5},{7,6},{8,7},{9,8},{10,9},{11,1... | collective-permute-start | bytes 18440 | tf_op jit(solution)/shard_map/while/body/eval_jaxpr/ppermute | solution.py:21
  45.1 4.3 %collective-permute-done.1 = bf16[4,2,1,384]{3,2,1,0:T(2,128)(2,1)S(1)} collective-permute-done((bf16[4,2,1,384]{3,2,1,0:T(2,128)(2,1)S(1)}, bf16[4,2,1,384]{3,2,1,0:T(2,128)(2,1)S(1)}, u32[]{:S(2)}, u32[]{:S(2)}) %collective-permute-start.1) | collective-permute-done | bytes 6176 | tf_op jit(solution)/shard_map/while/body/eval_jaxpr/ppermute | solution.py:21
  61.2 1.5 select_dynamic-update-slice_fusion.2
  62.7 5.5 %collective-permute-start.2 = (bf16[2,4,2,8,384]{4,3,2,1,0:T(8,128)(2,1)S(1)}, bf16[2,4,2,8,384]{4,3,2,1,0:T(8,128)(2,1)S(1)}, u32[]{:S(2)}, u32[]{:S(2)}) collective-permute-start(bf16[2,4,2,8,384]{4,3,2,1,0:T(8,128)(2,1)S(1)} %pad_maximum_fusion.3), channel_id=1, source_target_pairs={{0,64},{64,128},{128,192},{192,256},{256,320},{320,384},{384,448},... | collective-permute-start | bytes 294920 | tf_op jit(solution)/shard_map/while/body/eval_jaxpr/ppermute | solution.py:29
  68.2 1.6 collective-permute-done.2
  71.6 1.9 collective-permute-start
  73.5 3.4 %collective-permute-start.1 = (bf16[4,2,1,384]{3,2,1,0:T(2,128)(2,1)S(1)}, bf16[4,2,1,384]{3,2,1,0:T(2,128)(2,1)S(1)}, u32[]{:S(2)}, u32[]{:S(2)}) collective-permute-start(bf16[4,2,1,384]{3,2,1,0:T(2,128)(2,1)S(1)} %get-tuple-element.519), channel_id=1, source_target_pairs={{1,0},{2,1},{3,2},{4,3},{5,4},{6,5},{7,6},{8,7},{9,8},{10,9},{11,1... | collective-permute-start | bytes 18440 | tf_op jit(solution)/shard_map/while/body/eval_jaxpr/ppermute | solution.py:21
  77.0 4.3 %collective-permute-done.1 = bf16[4,2,1,384]{3,2,1,0:T(2,128)(2,1)S(1)} collective-permute-done((bf16[4,2,1,384]{3,2,1,0:T(2,128)(2,1)S(1)}, bf16[4,2,1,384]{3,2,1,0:T(2,128)(2,1)S(1)}, u32[]{:S(2)}, u32[]{:S(2)}) %collective-permute-start.1) | collective-permute-done | bytes 6176 | tf_op jit(solution)/shard_map/while/body/eval_jaxpr/ppermute | solution.py:21
  93.1 1.5 select_dynamic-update-slice_fusion.2
  94.6 5.5 %collective-permute-start.2 = (bf16[2,4,2,8,384]{4,3,2,1,0:T(8,128)(2,1)S(1)}, bf16[2,4,2,8,384]{4,3,2,1,0:T(8,128)(2,1)S(1)}, u32[]{:S(2)}, u32[]{:S(2)}) collective-permute-start(bf16[2,4,2,8,384]{4,3,2,1,0:T(8,128)(2,1)S(1)} %pad_maximum_fusion.3), channel_id=1, source_target_pairs={{0,64},{64,128},{128,192},{192,256},{256,320},{320,384},{384,448},... | collective-permute-start | bytes 294920 | tf_op jit(solution)/shard_map/while/body/eval_jaxpr/ppermute | solution.py:29
  100.1 1.6 collective-permute-done.2
  103.5 1.9 collective-permute-start
  105.4 3.4 %collective-permute-start.1 = (bf16[4,2,1,384]{3,2,1,0:T(2,128)(2,1)S(1)}, bf16[4,2,1,384]{3,2,1,0:T(2,128)(2,1)S(1)}, u32[]{:S(2)}, u32[]{:S(2)}) collective-permute-start(bf16[4,2,1,384]{3,2,1,0:T(2,128)(2,1)S(1)} %get-tuple-element.519), channel_id=1, source_target_pairs={{1,0},{2,1},{3,2},{4,3},{5,4},{6,5},{7,6},{8,7},{9,8},{10,9},{11,1... | collective-permute-start | bytes 18440 | tf_op jit(solution)/shard_map/while/body/eval_jaxpr/ppermute | solution.py:21
  108.9 4.3 %collective-permute-done.1 = bf16[4,2,1,384]{3,2,1,0:T(2,128)(2,1)S(1)} collective-permute-done((bf16[4,2,1,384]{3,2,1,0:T(2,128)(2,1)S(1)}, bf16[4,2,1,384]{3,2,1,0:T(2,128)(2,1)S(1)}, u32[]{:S(2)}, u32[]{:S(2)}) %collective-permute-start.1) | collective-permute-done | bytes 6176 | tf_op jit(solution)/shard_map/while/body/eval_jaxpr/ppermute | solution.py:21
  125.0 1.5 select_dynamic-update-slice_fusion.2
  126.5 5.5 %collective-permute-start.2 = (bf16[2,4,2,8,384]{4,3,2,1,0:T(8,128)(2,1)S(1)}, bf16[2,4,2,8,384]{4,3,2,1,0:T(8,128)(2,1)S(1)}, u32[]{:S(2)}, u32[]{:S(2)}) collective-permute-start(bf16[2,4,2,8,384]{4,3,2,1,0:T(8,128)(2,1)S(1)} %pad_maximum_fusion.3), channel_id=1, source_target_pairs={{0,64},{64,128},{128,192},{192,256},{256,320},{320,384},{384,448},... | collective-permute-start | bytes 294920 | tf_op jit(solution)/shard_map/while/body/eval_jaxpr/ppermute | solution.py:29
  132.0 1.6 collective-permute-done.2
  135.4 1.9 collective-permute-start
  137.3 3.4 %collective-permute-start.1 = (bf16[4,2,1,384]{3,2,1,0:T(2,128)(2,1)S(1)}, bf16[4,2,1,384]{3,2,1,0:T(2,128)(2,1)S(1)}, u32[]{:S(2)}, u32[]{:S(2)}) collective-permute-start(bf16[4,2,1,384]{3,2,1,0:T(2,128)(2,1)S(1)} %get-tuple-element.519), channel_id=1, source_target_pairs={{1,0},{2,1},{3,2},{4,3},{5,4},{6,5},{7,6},{8,7},{9,8},{10,9},{11,1... | collective-permute-start | bytes 18440 | tf_op jit(solution)/shard_map/while/body/eval_jaxpr/ppermute | solution.py:21
  140.8 4.3 %collective-permute-done.1 = bf16[4,2,1,384]{3,2,1,0:T(2,128)(2,1)S(1)} collective-permute-done((bf16[4,2,1,384]{3,2,1,0:T(2,128)(2,1)S(1)}, bf16[4,2,1,384]{3,2,1,0:T(2,128)(2,1)S(1)}, u32[]{:S(2)}, u32[]{:S(2)}) %collective-permute-start.1) | collective-permute-done | bytes 6176 | tf_op jit(solution)/shard_map/while/body/eval_jaxpr/ppermute | solution.py:21
  146.9 1.4 convolution_add_fusion.15
  151.2 1.4 convolution_add_fusion.18
  152.6 1.4 convolution_add_fusion.19
  156.9 1.5 select_dynamic-update-slice_fusion.2
  158.4 5.5 %collective-permute-start.2 = (bf16[2,4,2,8,384]{4,3,2,1,0:T(8,128)(2,1)S(1)}, bf16[2,4,2,8,384]{4,3,2,1,0:T(8,128)(2,1)S(1)}, u32[]{:S(2)}, u32[]{:S(2)}) collective-permute-start(bf16[2,4,2,8,384]{4,3,2,1,0:T(8,128)(2,1)S(1)} %pad_maximum_fusion.3), channel_id=1, source_target_pairs={{0,64},{64,128},{128,192},{192,256},{256,320},{320,384},{384,448},... | collective-permute-start | bytes 294920 | tf_op jit(solution)/shard_map/while/body/eval_jaxpr/ppermute | solution.py:29
  163.9 1.6 collective-permute-done.2
  167.3 1.9 collective-permute-start
  169.2 3.4 %collective-permute-start.1 = (bf16[4,2,1,384]{3,2,1,0:T(2,128)(2,1)S(1)}, bf16[4,2,1,384]{3,2,1,0:T(2,128)(2,1)S(1)}, u32[]{:S(2)}, u32[]{:S(2)}) collective-permute-start(bf16[4,2,1,384]{3,2,1,0:T(2,128)(2,1)S(1)} %get-tuple-element.519), channel_id=1, source_target_pairs={{1,0},{2,1},{3,2},{4,3},{5,4},{6,5},{7,6},{8,7},{9,8},{10,9},{11,1... | collective-permute-start | bytes 18440 | tf_op jit(solution)/shard_map/while/body/eval_jaxpr/ppermute | solution.py:21
  172.7 4.3 %collective-permute-done.1 = bf16[4,2,1,384]{3,2,1,0:T(2,128)(2,1)S(1)} collective-permute-done((bf16[4,2,1,384]{3,2,1,0:T(2,128)(2,1)S(1)}, bf16[4,2,1,384]{3,2,1,0:T(2,128)(2,1)S(1)}, u32[]{:S(2)}, u32[]{:S(2)}) %collective-permute-start.1) | collective-permute-done | bytes 6176 | tf_op jit(solution)/shard_map/while/body/eval_jaxpr/ppermute | solution.py:21
  178.8 1.4 convolution_add_fusion.15
  188.8 1.5 select_dynamic-update-slice_fusion.2
  190.3 5.5 %collective-permute-start.2 = (bf16[2,4,2,8,384]{4,3,2,1,0:T(8,128)(2,1)S(1)}, bf16[2,4,2,8,384]{4,3,2,1,0:T(8,128)(2,1)S(1)}, u32[]{:S(2)}, u32[]{:S(2)}) collective-permute-start(bf16[2,4,2,8,384]{4,3,2,1,0:T(8,128)(2,1)S(1)} %pad_maximum_fusion.3), channel_id=1, source_target_pairs={{0,64},{64,128},{128,192},{192,256},{256,320},{320,384},{384,448},... | collective-permute-start | bytes 294920 | tf_op jit(solution)/shard_map/while/body/eval_jaxpr/ppermute | solution.py:29
  195.8 1.6 collective-permute-done.2
  199.1 1.9 collective-permute-start
  201.1 3.4 %collective-permute-start.1 = (bf16[4,2,1,384]{3,2,1,0:T(2,128)(2,1)S(1)}, bf16[4,2,1,384]{3,2,1,0:T(2,128)(2,1)S(1)}, u32[]{:S(2)}, u32[]{:S(2)}) collective-permute-start(bf16[4,2,1,384]{3,2,1,0:T(2,128)(2,1)S(1)} %get-tuple-element.519), channel_id=1, source_target_pairs={{1,0},{2,1},{3,2},{4,3},{5,4},{6,5},{7,6},{8,7},{9,8},{10,9},{11,1... | collective-permute-start | bytes 18440 | tf_op jit(solution)/shard_map/while/body/eval_jaxpr/ppermute | solution.py:21
  204.6 4.3 %collective-permute-done.1 = bf16[4,2,1,384]{3,2,1,0:T(2,128)(2,1)S(1)} collective-permute-done((bf16[4,2,1,384]{3,2,1,0:T(2,128)(2,1)S(1)}, bf16[4,2,1,384]{3,2,1,0:T(2,128)(2,1)S(1)}, u32[]{:S(2)}, u32[]{:S(2)}) %collective-permute-start.1) | collective-permute-done | bytes 6176 | tf_op jit(solution)/shard_map/while/body/eval_jaxpr/ppermute | solution.py:21
  220.7 1.5 select_dynamic-update-slice_fusion.2
  222.2 5.5 %collective-permute-start.2 = (bf16[2,4,2,8,384]{4,3,2,1,0:T(8,128)(2,1)S(1)}, bf16[2,4,2,8,384]{4,3,2,1,0:T(8,128)(2,1)S(1)}, u32[]{:S(2)}, u32[]{:S(2)}) collective-permute-start(bf16[2,4,2,8,384]{4,3,2,1,0:T(8,128)(2,1)S(1)} %pad_maximum_fusion.3), channel_id=1, source_target_pairs={{0,64},{64,128},{128,192},{192,256},{256,320},{320,384},{384,448},... | collective-permute-start | bytes 294920 | tf_op jit(solution)/shard_map/while/body/eval_jaxpr/ppermute | solution.py:29
  227.7 1.6 collective-permute-done.2
  231.0 1.9 collective-permute-start
  233.0 3.4 %collective-permute-start.1 = (bf16[4,2,1,384]{3,2,1,0:T(2,128)(2,1)S(1)}, bf16[4,2,1,384]{3,2,1,0:T(2,128)(2,1)S(1)}, u32[]{:S(2)}, u32[]{:S(2)}) collective-permute-start(bf16[4,2,1,384]{3,2,1,0:T(2,128)(2,1)S(1)} %get-tuple-element.519), channel_id=1, source_target_pairs={{1,0},{2,1},{3,2},{4,3},{5,4},{6,5},{7,6},{8,7},{9,8},{10,9},{11,1... | collective-permute-start | bytes 18440 | tf_op jit(solution)/shard_map/while/body/eval_jaxpr/ppermute | solution.py:21
  236.4 4.3 %collective-permute-done.1 = bf16[4,2,1,384]{3,2,1,0:T(2,128)(2,1)S(1)} collective-permute-done((bf16[4,2,1,384]{3,2,1,0:T(2,128)(2,1)S(1)}, bf16[4,2,1,384]{3,2,1,0:T(2,128)(2,1)S(1)}, u32[]{:S(2)}, u32[]{:S(2)}) %collective-permute-start.1) | collective-permute-done | bytes 6176 | tf_op jit(solution)/shard_map/while/body/eval_jaxpr/ppermute | solution.py:21
  252.6 1.5 select_dynamic-update-slice_fusion.2
  254.1 5.5 %collective-permute-start.2 = (bf16[2,4,2,8,384]{4,3,2,1,0:T(8,128)(2,1)S(1)}, bf16[2,4,2,8,384]{4,3,2,1,0:T(8,128)(2,1)S(1)}, u32[]{:S(2)}, u32[]{:S(2)}) collective-permute-start(bf16[2,4,2,8,384]{4,3,2,1,0:T(8,128)(2,1)S(1)} %pad_maximum_fusion.3), channel_id=1, source_target_pairs={{0,64},{64,128},{128,192},{192,256},{256,320},{320,384},{384,448},... | collective-permute-start | bytes 294920 | tf_op jit(solution)/shard_map/while/body/eval_jaxpr/ppermute | solution.py:29
  259.5 1.6 collective-permute-done.2
  262.9 1.9 collective-permute-start
  264.9 3.4 %collective-permute-start.1 = (bf16[4,2,1,384]{3,2,1,0:T(2,128)(2,1)S(1)}, bf16[4,2,1,384]{3,2,1,0:T(2,128)(2,1)S(1)}, u32[]{:S(2)}, u32[]{:S(2)}) collective-permute-start(bf16[4,2,1,384]{3,2,1,0:T(2,128)(2,1)S(1)} %get-tuple-element.519), channel_id=1, source_target_pairs={{1,0},{2,1},{3,2},{4,3},{5,4},{6,5},{7,6},{8,7},{9,8},{10,9},{11,1... | collective-permute-start | bytes 18440 | tf_op jit(solution)/shard_map/while/body/eval_jaxpr/ppermute | solution.py:21
  268.3 4.3 %collective-permute-done.1 = bf16[4,2,1,384]{3,2,1,0:T(2,128)(2,1)S(1)} collective-permute-done((bf16[4,2,1,384]{3,2,1,0:T(2,128)(2,1)S(1)}, bf16[4,2,1,384]{3,2,1,0:T(2,128)(2,1)S(1)}, u32[]{:S(2)}, u32[]{:S(2)}) %collective-permute-start.1) | collective-permute-done | bytes 6176 | tf_op jit(solution)/shard_map/while/body/eval_jaxpr/ppermute | solution.py:21
  284.5 1.5 select_dynamic-update-slice_fusion.2
  286.0 5.5 %collective-permute-start.2 = (bf16[2,4,2,8,384]{4,3,2,1,0:T(8,128)(2,1)S(1)}, bf16[2,4,2,8,384]{4,3,2,1,0:T(8,128)(2,1)S(1)}, u32[]{:S(2)}, u32[]{:S(2)}) collective-permute-start(bf16[2,4,2,8,384]{4,3,2,1,0:T(8,128)(2,1)S(1)} %pad_maximum_fusion.3), channel_id=1, source_target_pairs={{0,64},{64,128},{128,192},{192,256},{256,320},{320,384},{384,448},... | collective-permute-start | bytes 294920 | tf_op jit(solution)/shard_map/while/body/eval_jaxpr/ppermute | solution.py:29
  291.4 1.6 collective-permute-done.2
  293.1 15.0 %all-gather = bf16[64,2,8,384]{3,2,1,0:T(8,128)(2,1)S(1)} all-gather(bf16[8,2,8,384]{3,2,1,0:T(8,128)(2,1)S(1)} %broadcast_select_fusion.1), channel_id=2, replica_groups=mesh['section'=8,'tile'=64] {'section'}, dimensions={0}, use_global_device_ids=true | all-gather | bytes 884736 | tf_op jit(solution)/shard_map/all_gather | solution.py:10
  (207 shorter events, 113.7 us)
Async XLA Ops:
  5.6 12.2 %collective-permute-start = (bf16[4,2,1,384]{3,2,1,0:T(2,128)(2,1)S(1)}, bf16[4,2,1,384]{3,2,1,0:T(2,128)(2,1)S(1)}, u32[]{:S(2)}, u32[]{:S(2)}) collective-permute-start(bf16[4,2,1,384]{3,2,1,0:T(2,128)(2,1)S(1)} %get-tuple-element.518), channel_id=1, source_target_pairs={{0,1},{1,2},{2,3},{3,4},{4,5},{5,6},{6,7},{7,8},{8,9},{9,10},{10,1... | collective-permute-start | bytes 18440 | tf_op jit(solution)/shard_map/while/body/eval_jaxpr/ppermute | solution.py:18
  10.1 7.8 %collective-permute-start.1 = (bf16[4,2,1,384]{3,2,1,0:T(2,128)(2,1)S(1)}, bf16[4,2,1,384]{3,2,1,0:T(2,128)(2,1)S(1)}, u32[]{:S(2)}, u32[]{:S(2)}) collective-permute-start(bf16[4,2,1,384]{3,2,1,0:T(2,128)(2,1)S(1)} %get-tuple-element.519), channel_id=1, source_target_pairs={{1,0},{2,1},{3,2},{4,3},{5,4},{6,5},{7,6},{8,7},{9,8},{10,9},{11,1... | collective-permute-start | bytes 18440 | tf_op jit(solution)/shard_map/while/body/eval_jaxpr/ppermute | solution.py:21
  31.2 6.7 %collective-permute-start.2 = (bf16[2,4,2,8,384]{4,3,2,1,0:T(8,128)(2,1)S(1)}, bf16[2,4,2,8,384]{4,3,2,1,0:T(8,128)(2,1)S(1)}, u32[]{:S(2)}, u32[]{:S(2)}) collective-permute-start(bf16[2,4,2,8,384]{4,3,2,1,0:T(8,128)(2,1)S(1)} %pad_maximum_fusion.3), channel_id=1, source_target_pairs={{0,64},{64,128},{128,192},{192,256},{256,320},{320,384},{384,448},... | collective-permute-start | bytes 294920 | tf_op jit(solution)/shard_map/while/body/eval_jaxpr/ppermute | solution.py:29
  39.7 9.7 %collective-permute-start = (bf16[4,2,1,384]{3,2,1,0:T(2,128)(2,1)S(1)}, bf16[4,2,1,384]{3,2,1,0:T(2,128)(2,1)S(1)}, u32[]{:S(2)}, u32[]{:S(2)}) collective-permute-start(bf16[4,2,1,384]{3,2,1,0:T(2,128)(2,1)S(1)} %get-tuple-element.518), channel_id=1, source_target_pairs={{0,1},{1,2},{2,3},{3,4},{4,5},{5,6},{6,7},{7,8},{8,9},{9,10},{10,1... | collective-permute-start | bytes 18440 | tf_op jit(solution)/shard_map/while/body/eval_jaxpr/ppermute | solution.py:18
  41.6 7.8 %collective-permute-start.1 = (bf16[4,2,1,384]{3,2,1,0:T(2,128)(2,1)S(1)}, bf16[4,2,1,384]{3,2,1,0:T(2,128)(2,1)S(1)}, u32[]{:S(2)}, u32[]{:S(2)}) collective-permute-start(bf16[4,2,1,384]{3,2,1,0:T(2,128)(2,1)S(1)} %get-tuple-element.519), channel_id=1, source_target_pairs={{1,0},{2,1},{3,2},{4,3},{5,4},{6,5},{7,6},{8,7},{9,8},{10,9},{11,1... | collective-permute-start | bytes 18440 | tf_op jit(solution)/shard_map/while/body/eval_jaxpr/ppermute | solution.py:21
  62.7 7.1 %collective-permute-start.2 = (bf16[2,4,2,8,384]{4,3,2,1,0:T(8,128)(2,1)S(1)}, bf16[2,4,2,8,384]{4,3,2,1,0:T(8,128)(2,1)S(1)}, u32[]{:S(2)}, u32[]{:S(2)}) collective-permute-start(bf16[2,4,2,8,384]{4,3,2,1,0:T(8,128)(2,1)S(1)} %pad_maximum_fusion.3), channel_id=1, source_target_pairs={{0,64},{64,128},{128,192},{192,256},{256,320},{320,384},{384,448},... | collective-permute-start | bytes 294920 | tf_op jit(solution)/shard_map/while/body/eval_jaxpr/ppermute | solution.py:29
  71.6 9.7 %collective-permute-start = (bf16[4,2,1,384]{3,2,1,0:T(2,128)(2,1)S(1)}, bf16[4,2,1,384]{3,2,1,0:T(2,128)(2,1)S(1)}, u32[]{:S(2)}, u32[]{:S(2)}) collective-permute-start(bf16[4,2,1,384]{3,2,1,0:T(2,128)(2,1)S(1)} %get-tuple-element.518), channel_id=1, source_target_pairs={{0,1},{1,2},{2,3},{3,4},{4,5},{5,6},{6,7},{7,8},{8,9},{9,10},{10,1... | collective-permute-start | bytes 18440 | tf_op jit(solution)/shard_map/while/body/eval_jaxpr/ppermute | solution.py:18
  73.5 7.8 %collective-permute-start.1 = (bf16[4,2,1,384]{3,2,1,0:T(2,128)(2,1)S(1)}, bf16[4,2,1,384]{3,2,1,0:T(2,128)(2,1)S(1)}, u32[]{:S(2)}, u32[]{:S(2)}) collective-permute-start(bf16[4,2,1,384]{3,2,1,0:T(2,128)(2,1)S(1)} %get-tuple-element.519), channel_id=1, source_target_pairs={{1,0},{2,1},{3,2},{4,3},{5,4},{6,5},{7,6},{8,7},{9,8},{10,9},{11,1... | collective-permute-start | bytes 18440 | tf_op jit(solution)/shard_map/while/body/eval_jaxpr/ppermute | solution.py:21
  94.6 7.1 %collective-permute-start.2 = (bf16[2,4,2,8,384]{4,3,2,1,0:T(8,128)(2,1)S(1)}, bf16[2,4,2,8,384]{4,3,2,1,0:T(8,128)(2,1)S(1)}, u32[]{:S(2)}, u32[]{:S(2)}) collective-permute-start(bf16[2,4,2,8,384]{4,3,2,1,0:T(8,128)(2,1)S(1)} %pad_maximum_fusion.3), channel_id=1, source_target_pairs={{0,64},{64,128},{128,192},{192,256},{256,320},{320,384},{384,448},... | collective-permute-start | bytes 294920 | tf_op jit(solution)/shard_map/while/body/eval_jaxpr/ppermute | solution.py:29
  103.5 9.7 %collective-permute-start = (bf16[4,2,1,384]{3,2,1,0:T(2,128)(2,1)S(1)}, bf16[4,2,1,384]{3,2,1,0:T(2,128)(2,1)S(1)}, u32[]{:S(2)}, u32[]{:S(2)}) collective-permute-start(bf16[4,2,1,384]{3,2,1,0:T(2,128)(2,1)S(1)} %get-tuple-element.518), channel_id=1, source_target_pairs={{0,1},{1,2},{2,3},{3,4},{4,5},{5,6},{6,7},{7,8},{8,9},{9,10},{10,1... | collective-permute-start | bytes 18440 | tf_op jit(solution)/shard_map/while/body/eval_jaxpr/ppermute | solution.py:18
  105.4 7.8 %collective-permute-start.1 = (bf16[4,2,1,384]{3,2,1,0:T(2,128)(2,1)S(1)}, bf16[4,2,1,384]{3,2,1,0:T(2,128)(2,1)S(1)}, u32[]{:S(2)}, u32[]{:S(2)}) collective-permute-start(bf16[4,2,1,384]{3,2,1,0:T(2,128)(2,1)S(1)} %get-tuple-element.519), channel_id=1, source_target_pairs={{1,0},{2,1},{3,2},{4,3},{5,4},{6,5},{7,6},{8,7},{9,8},{10,9},{11,1... | collective-permute-start | bytes 18440 | tf_op jit(solution)/shard_map/while/body/eval_jaxpr/ppermute | solution.py:21
  126.5 7.1 %collective-permute-start.2 = (bf16[2,4,2,8,384]{4,3,2,1,0:T(8,128)(2,1)S(1)}, bf16[2,4,2,8,384]{4,3,2,1,0:T(8,128)(2,1)S(1)}, u32[]{:S(2)}, u32[]{:S(2)}) collective-permute-start(bf16[2,4,2,8,384]{4,3,2,1,0:T(8,128)(2,1)S(1)} %pad_maximum_fusion.3), channel_id=1, source_target_pairs={{0,64},{64,128},{128,192},{192,256},{256,320},{320,384},{384,448},... | collective-permute-start | bytes 294920 | tf_op jit(solution)/shard_map/while/body/eval_jaxpr/ppermute | solution.py:29
  135.4 9.7 %collective-permute-start = (bf16[4,2,1,384]{3,2,1,0:T(2,128)(2,1)S(1)}, bf16[4,2,1,384]{3,2,1,0:T(2,128)(2,1)S(1)}, u32[]{:S(2)}, u32[]{:S(2)}) collective-permute-start(bf16[4,2,1,384]{3,2,1,0:T(2,128)(2,1)S(1)} %get-tuple-element.518), channel_id=1, source_target_pairs={{0,1},{1,2},{2,3},{3,4},{4,5},{5,6},{6,7},{7,8},{8,9},{9,10},{10,1... | collective-permute-start | bytes 18440 | tf_op jit(solution)/shard_map/while/body/eval_jaxpr/ppermute | solution.py:18
  137.3 7.8 %collective-permute-start.1 = (bf16[4,2,1,384]{3,2,1,0:T(2,128)(2,1)S(1)}, bf16[4,2,1,384]{3,2,1,0:T(2,128)(2,1)S(1)}, u32[]{:S(2)}, u32[]{:S(2)}) collective-permute-start(bf16[4,2,1,384]{3,2,1,0:T(2,128)(2,1)S(1)} %get-tuple-element.519), channel_id=1, source_target_pairs={{1,0},{2,1},{3,2},{4,3},{5,4},{6,5},{7,6},{8,7},{9,8},{10,9},{11,1... | collective-permute-start | bytes 18440 | tf_op jit(solution)/shard_map/while/body/eval_jaxpr/ppermute | solution.py:21
  158.4 7.1 %collective-permute-start.2 = (bf16[2,4,2,8,384]{4,3,2,1,0:T(8,128)(2,1)S(1)}, bf16[2,4,2,8,384]{4,3,2,1,0:T(8,128)(2,1)S(1)}, u32[]{:S(2)}, u32[]{:S(2)}) collective-permute-start(bf16[2,4,2,8,384]{4,3,2,1,0:T(8,128)(2,1)S(1)} %pad_maximum_fusion.3), channel_id=1, source_target_pairs={{0,64},{64,128},{128,192},{192,256},{256,320},{320,384},{384,448},... | collective-permute-start | bytes 294920 | tf_op jit(solution)/shard_map/while/body/eval_jaxpr/ppermute | solution.py:29
  167.3 9.7 %collective-permute-start = (bf16[4,2,1,384]{3,2,1,0:T(2,128)(2,1)S(1)}, bf16[4,2,1,384]{3,2,1,0:T(2,128)(2,1)S(1)}, u32[]{:S(2)}, u32[]{:S(2)}) collective-permute-start(bf16[4,2,1,384]{3,2,1,0:T(2,128)(2,1)S(1)} %get-tuple-element.518), channel_id=1, source_target_pairs={{0,1},{1,2},{2,3},{3,4},{4,5},{5,6},{6,7},{7,8},{8,9},{9,10},{10,1... | collective-permute-start | bytes 18440 | tf_op jit(solution)/shard_map/while/body/eval_jaxpr/ppermute | solution.py:18
  169.2 7.8 %collective-permute-start.1 = (bf16[4,2,1,384]{3,2,1,0:T(2,128)(2,1)S(1)}, bf16[4,2,1,384]{3,2,1,0:T(2,128)(2,1)S(1)}, u32[]{:S(2)}, u32[]{:S(2)}) collective-permute-start(bf16[4,2,1,384]{3,2,1,0:T(2,128)(2,1)S(1)} %get-tuple-element.519), channel_id=1, source_target_pairs={{1,0},{2,1},{3,2},{4,3},{5,4},{6,5},{7,6},{8,7},{9,8},{10,9},{11,1... | collective-permute-start | bytes 18440 | tf_op jit(solution)/shard_map/while/body/eval_jaxpr/ppermute | solution.py:21
  190.3 7.1 %collective-permute-start.2 = (bf16[2,4,2,8,384]{4,3,2,1,0:T(8,128)(2,1)S(1)}, bf16[2,4,2,8,384]{4,3,2,1,0:T(8,128)(2,1)S(1)}, u32[]{:S(2)}, u32[]{:S(2)}) collective-permute-start(bf16[2,4,2,8,384]{4,3,2,1,0:T(8,128)(2,1)S(1)} %pad_maximum_fusion.3), channel_id=1, source_target_pairs={{0,64},{64,128},{128,192},{192,256},{256,320},{320,384},{384,448},... | collective-permute-start | bytes 294920 | tf_op jit(solution)/shard_map/while/body/eval_jaxpr/ppermute | solution.py:29
  199.1 9.7 %collective-permute-start = (bf16[4,2,1,384]{3,2,1,0:T(2,128)(2,1)S(1)}, bf16[4,2,1,384]{3,2,1,0:T(2,128)(2,1)S(1)}, u32[]{:S(2)}, u32[]{:S(2)}) collective-permute-start(bf16[4,2,1,384]{3,2,1,0:T(2,128)(2,1)S(1)} %get-tuple-element.518), channel_id=1, source_target_pairs={{0,1},{1,2},{2,3},{3,4},{4,5},{5,6},{6,7},{7,8},{8,9},{9,10},{10,1... | collective-permute-start | bytes 18440 | tf_op jit(solution)/shard_map/while/body/eval_jaxpr/ppermute | solution.py:18
  201.1 7.8 %collective-permute-start.1 = (bf16[4,2,1,384]{3,2,1,0:T(2,128)(2,1)S(1)}, bf16[4,2,1,384]{3,2,1,0:T(2,128)(2,1)S(1)}, u32[]{:S(2)}, u32[]{:S(2)}) collective-permute-start(bf16[4,2,1,384]{3,2,1,0:T(2,128)(2,1)S(1)} %get-tuple-element.519), channel_id=1, source_target_pairs={{1,0},{2,1},{3,2},{4,3},{5,4},{6,5},{7,6},{8,7},{9,8},{10,9},{11,1... | collective-permute-start | bytes 18440 | tf_op jit(solution)/shard_map/while/body/eval_jaxpr/ppermute | solution.py:21
  222.2 7.1 %collective-permute-start.2 = (bf16[2,4,2,8,384]{4,3,2,1,0:T(8,128)(2,1)S(1)}, bf16[2,4,2,8,384]{4,3,2,1,0:T(8,128)(2,1)S(1)}, u32[]{:S(2)}, u32[]{:S(2)}) collective-permute-start(bf16[2,4,2,8,384]{4,3,2,1,0:T(8,128)(2,1)S(1)} %pad_maximum_fusion.3), channel_id=1, source_target_pairs={{0,64},{64,128},{128,192},{192,256},{256,320},{320,384},{384,448},... | collective-permute-start | bytes 294920 | tf_op jit(solution)/shard_map/while/body/eval_jaxpr/ppermute | solution.py:29
  231.0 9.7 %collective-permute-start = (bf16[4,2,1,384]{3,2,1,0:T(2,128)(2,1)S(1)}, bf16[4,2,1,384]{3,2,1,0:T(2,128)(2,1)S(1)}, u32[]{:S(2)}, u32[]{:S(2)}) collective-permute-start(bf16[4,2,1,384]{3,2,1,0:T(2,128)(2,1)S(1)} %get-tuple-element.518), channel_id=1, source_target_pairs={{0,1},{1,2},{2,3},{3,4},{4,5},{5,6},{6,7},{7,8},{8,9},{9,10},{10,1... | collective-permute-start | bytes 18440 | tf_op jit(solution)/shard_map/while/body/eval_jaxpr/ppermute | solution.py:18
  233.0 7.8 %collective-permute-start.1 = (bf16[4,2,1,384]{3,2,1,0:T(2,128)(2,1)S(1)}, bf16[4,2,1,384]{3,2,1,0:T(2,128)(2,1)S(1)}, u32[]{:S(2)}, u32[]{:S(2)}) collective-permute-start(bf16[4,2,1,384]{3,2,1,0:T(2,128)(2,1)S(1)} %get-tuple-element.519), channel_id=1, source_target_pairs={{1,0},{2,1},{3,2},{4,3},{5,4},{6,5},{7,6},{8,7},{9,8},{10,9},{11,1... | collective-permute-start | bytes 18440 | tf_op jit(solution)/shard_map/while/body/eval_jaxpr/ppermute | solution.py:21
  254.1 7.1 %collective-permute-start.2 = (bf16[2,4,2,8,384]{4,3,2,1,0:T(8,128)(2,1)S(1)}, bf16[2,4,2,8,384]{4,3,2,1,0:T(8,128)(2,1)S(1)}, u32[]{:S(2)}, u32[]{:S(2)}) collective-permute-start(bf16[2,4,2,8,384]{4,3,2,1,0:T(8,128)(2,1)S(1)} %pad_maximum_fusion.3), channel_id=1, source_target_pairs={{0,64},{64,128},{128,192},{192,256},{256,320},{320,384},{384,448},... | collective-permute-start | bytes 294920 | tf_op jit(solution)/shard_map/while/body/eval_jaxpr/ppermute | solution.py:29
  262.9 9.7 %collective-permute-start = (bf16[4,2,1,384]{3,2,1,0:T(2,128)(2,1)S(1)}, bf16[4,2,1,384]{3,2,1,0:T(2,128)(2,1)S(1)}, u32[]{:S(2)}, u32[]{:S(2)}) collective-permute-start(bf16[4,2,1,384]{3,2,1,0:T(2,128)(2,1)S(1)} %get-tuple-element.518), channel_id=1, source_target_pairs={{0,1},{1,2},{2,3},{3,4},{4,5},{5,6},{6,7},{7,8},{8,9},{9,10},{10,1... | collective-permute-start | bytes 18440 | tf_op jit(solution)/shard_map/while/body/eval_jaxpr/ppermute | solution.py:18
  264.9 7.8 %collective-permute-start.1 = (bf16[4,2,1,384]{3,2,1,0:T(2,128)(2,1)S(1)}, bf16[4,2,1,384]{3,2,1,0:T(2,128)(2,1)S(1)}, u32[]{:S(2)}, u32[]{:S(2)}) collective-permute-start(bf16[4,2,1,384]{3,2,1,0:T(2,128)(2,1)S(1)} %get-tuple-element.519), channel_id=1, source_target_pairs={{1,0},{2,1},{3,2},{4,3},{5,4},{6,5},{7,6},{8,7},{9,8},{10,9},{11,1... | collective-permute-start | bytes 18440 | tf_op jit(solution)/shard_map/while/body/eval_jaxpr/ppermute | solution.py:21
  286.0 7.1 %collective-permute-start.2 = (bf16[2,4,2,8,384]{4,3,2,1,0:T(8,128)(2,1)S(1)}, bf16[2,4,2,8,384]{4,3,2,1,0:T(8,128)(2,1)S(1)}, u32[]{:S(2)}, u32[]{:S(2)}) collective-permute-start(bf16[2,4,2,8,384]{4,3,2,1,0:T(8,128)(2,1)S(1)} %pad_maximum_fusion.3), channel_id=1, source_target_pairs={{0,64},{64,128},{128,192},{192,256},{256,320},{320,384},{384,448},... | collective-permute-start | bytes 294920 | tf_op jit(solution)/shard_map/while/body/eval_jaxpr/ppermute | solution.py:29
